TPU v7x, 512 devices: a whole 4x4x16 slice. The times are simulated.
512 devices in a mesh: fsdp: 128 (over z, y, core), seq: 4 (over x).
Axes of the slice: x: 4, y: 4, z: 16, core: 2. Of those that a mesh axis runs over, the one named last changes fastest.
Arguments:
- tokens: bfloat16 [128, 512, 8192], P('fsdp', 'seq'), may hold values from -6 to 6
- queries: bfloat16 [128, 512, 8192], P('fsdp', None, 'seq'), may hold values from -6 to 6
- key_weight: bfloat16 [8192, 1024], P('fsdp', 'seq'), may hold values from -1 to 1
- u_factor: float32 [8192, 64], P('fsdp'), may hold values from -6 to 6
- v_factor: float32 [1024, 64], replicated, may hold values from -6 to 6
Outputs:
- update: float32 [8192, 1024], P('fsdp')
- losses: float32 [2], replicated
All inputs are finite; a program needn't handle non-finite values.
Results may differ from a plain program's by a relative error of at most 0.0003.
Values may be sent and summed in bfloat16 or wider, within the bound.
No kernel may reach another device: no remote copies, remote signals or barrier semaphores. Data moves between devices by JAX's collectives and lax.ppermute only.
A program may use at most 64 MiB of HBM per device.

v0:
```python
import math
import jax
import jax.numpy as jnp
from jax import lax
from jax.sharding import PartitionSpec as P

D = 8192
HQ = 64
HD = 128
R = 64
KD = 1024
GROUP = 8


def highest(left, right):
    return jnp.dot(left, right, precision=lax.Precision.HIGHEST, preferred_element_type=jnp.float32)


def solve_rows(rows, gram):
    lower = jnp.linalg.cholesky(gram)
    return lax.linalg.triangular_solve(lower, rows, left_side=False, lower=True, transpose_a=True)


def orthonormal(factor):
    for turn in range(2):
        factor = solve_rows(factor, highest(factor.T, factor))
    return factor


def orthonormal_map(factor):
    gram = highest(factor.T, factor)
    eye = jnp.eye(gram.shape[0], dtype=gram.dtype)
    first = lax.linalg.triangular_solve(
        jnp.linalg.cholesky(gram), eye, left_side=False, lower=True, transpose_a=True
    )
    second_gram = highest(first.T, highest(gram, first))
    second = lax.linalg.triangular_solve(
        jnp.linalg.cholesky(second_gram), eye, left_side=False, lower=True, transpose_a=True
    )
    return highest(factor, highest(first, second))


def split3(values):
    hi = lax.reduce_precision(values, exponent_bits=8, mantissa_bits=7)
    rest = values - hi
    mid = lax.reduce_precision(rest, exponent_bits=8, mantissa_bits=7)
    lo = rest - mid
    return [piece.astype(jnp.bfloat16) for piece in (hi, mid, lo)]


def total_over(values, axis):
    n = lax.axis_size(axis)
    spread = jnp.broadcast_to(values[None], (n,) + values.shape)
    return jnp.sum(lax.all_to_all(spread, axis, 0, 0, tiled=True), axis=0)


def local(tokens, queries, key_weight, u_factor, v_factor):
    n_seq = lax.axis_size("seq")
    me_seq = lax.axis_index("seq")
    me_fsdp = lax.axis_index("fsdp")
    slice_width = key_weight.shape[1]
    rows = u_factor.shape[0]
    packed = jnp.concatenate([key_weight] + split3(u_factor), axis=1)
    whole = lax.all_gather(packed, "fsdp", axis=0, tiled=True)
    x_local = tokens[0]
    chunk = x_local.shape[0]
    chunks = [x_local]
    for shift in range(1, n_seq):
        chunks.append(
            lax.ppermute(x_local, "seq", [(i, (i + shift) % n_seq) for i in range(n_seq)])
        )
    q_v = orthonormal(v_factor)
    weight_piece = whole[:, :slice_width]
    r = u_factor.shape[1]
    u_whole = (
        whole[:, slice_width : slice_width + r].astype(jnp.float32)
        + whole[:, slice_width + r : slice_width + 2 * r].astype(jnp.float32)
        + whole[:, slice_width + 2 * r :].astype(jnp.float32)
    )
    q_u = orthonormal_map(lax.optimization_barrier(u_whole))
    q_low = q_u.astype(jnp.bfloat16)
    both = jnp.concatenate([weight_piece, q_low], axis=1)
    col_start = me_seq * slice_width
    v_slice = lax.dynamic_slice_in_dim(q_v, col_start, slice_width, 0)
    prod = jnp.dot(jnp.concatenate(chunks, axis=0), both, preferred_element_type=jnp.float32)
    base = prod[:, :slice_width]
    side = prod[:, slice_width:]
    offset = 2.0 * highest(side, v_slice.T)
    keys = jnp.stack([base + offset, base - offset]).astype(jnp.bfloat16)
    length = keys.shape[1]
    block = (me_seq - jnp.arange(n_seq)) % n_seq
    key_pos = (block[:, None] * chunk + jnp.arange(chunk)[None, :]).reshape(length)
    local_kv = slice_width // HD
    query_rows = queries[0]
    query_heads = query_rows.reshape(length, local_kv, GROUP, HD).transpose(1, 2, 0, 3)
    key_heads = keys.reshape(2, length, local_kv, HD).transpose(2, 0, 1, 3)
    places = jnp.arange(length)
    causal = places[:, None] >= key_pos[None, :]
    factor_scale = 1.0 / math.sqrt(HD)

    def one_query_head(query_one, key_one):
        scores = (
            jnp.einsum("td,npd->ntp", query_one, key_one, preferred_element_type=jnp.float32)
            * factor_scale
        )
        scores = jnp.where(causal[None], scores, -1e30)
        top = jnp.max(scores, axis=-1)
        total = jnp.sum(jnp.where(causal[None], jnp.exp(scores - top[..., None]), 0.0), axis=-1)
        return jnp.sum(top + jnp.log(total), axis=1)

    def one_key_head(pair):
        group_queries, key_one = pair
        return jnp.sum(
            lax.map(lambda query_one: one_query_head(query_one, key_one), group_queries), axis=0
        )

    partial_sums = jnp.sum(lax.map(one_key_head, (query_heads, key_heads)), axis=0)
    sums = total_over(total_over(partial_sums, "fsdp"), "seq")
    losses = sums / (lax.axis_size("fsdp") * length * HQ)
    unit = math.sqrt(D * KD / R)
    u_rows = lax.dynamic_slice_in_dim(q_u, me_fsdp * rows, rows, 0)
    update = unit * highest(u_rows, q_v.T)
    return (update, losses)


def solution(mesh):
    in_specs = (
        P("fsdp", "seq", None),
        P("fsdp", None, "seq"),
        P("fsdp", "seq"),
        P("fsdp", None),
        P(),
    )
    out_specs = (P("fsdp", None), P())
    return jax.shard_map(local, mesh=mesh, in_specs=in_specs, out_specs=out_specs, check_vma=False)
```

profile of v0, /device:TPU:1, one launch (start us, length us, event | category | flops | bytes accessed | tf_op | source)
XLA Modules:
  0.0 288.8 jit_solution(2902003976088465910)
XLA Ops:
  9.7 3.9 %collective-permute-start = (bf16[128,8192]{1,0:T(8,128)(2,1)}, bf16[128,8192]{1,0:T(8,128)(2,1)}, u32[]{:S(2)}, u32[]{:S(2)}) collective-permute-start(bf16[128,8192]{1,0:T(8,128)(2,1)} %bitcast.114), channel_id=1, source_target_pairs={{0,1},{1,2},{2,3},{3,0},{4,5},{5,6},{6,7},{7,4},{8,9},{9,10},{10,1... | collective-permute-start | bytes 6291464 | tf_op jit(solution)/shard_map/ppermute | solution.py:70
  13.6 4.4 %collective-permute-start.1 = (bf16[128,8192]{1,0:T(8,128)(2,1)}, bf16[128,8192]{1,0:T(8,128)(2,1)}, u32[]{:S(2)}, u32[]{:S(2)}) collective-permute-start(bf16[128,8192]{1,0:T(8,128)(2,1)} %bitcast.115), channel_id=1, source_target_pairs={{0,2},{1,3},{2,0},{3,1},{4,6},{5,7},{6,4},{7,5},{8,10},{9,11},{10,... | collective-permute-start | bytes 6291464 | tf_op jit(solution)/shard_map/ppermute | solution.py:70
  18.0 3.1 %collective-permute-start.2 = (bf16[128,8192]{1,0:T(8,128)(2,1)}, bf16[128,8192]{1,0:T(8,128)(2,1)}, u32[]{:S(2)}, u32[]{:S(2)}) collective-permute-start(bf16[128,8192]{1,0:T(8,128)(2,1)} %bitcast.116), channel_id=1, source_target_pairs={{0,3},{1,0},{2,1},{3,2},{4,7},{5,4},{6,5},{7,6},{8,11},{9,8},{10,9... | collective-permute-start | bytes 6291464 | tf_op jit(solution)/shard_map/ppermute | solution.py:70
  21.5 5.8 %cholesky.96 = f32[64,64]{1,0:T(8,128)S(1)} custom-call(f32[64,64]{1,0:T(8,128)S(1)} %fusion.32), custom_call_target="Cholesky" | custom-call | tf_op jit(solution)/shard_map/jit(cholesky)/cholesky | solution.py:20
  28.7 4.9 %custom-call.12 = f32[1,64,64]{1,2,0:T(8,128)S(1)} custom-call(f32[1,64,64]{2,1,0:T(8,128)S(1)} %fusion.26), custom_call_target="InvertDiagBlocksLowerTriangular" | custom-call | tf_op jit(solution)/shard_map/triangular_solve/custom-call.2 | solution.py:21
  34.5 5.9 %cholesky.107 = f32[64,64]{1,0:T(8,128)S(1)} custom-call(f32[64,64]{1,0:T(8,128)S(1)} %fusion.30), custom_call_target="Cholesky" | custom-call | tf_op jit(solution)/shard_map/jit(cholesky)/cholesky | solution.py:20
  41.7 4.9 %custom-call.13 = f32[1,64,64]{1,2,0:T(8,128)S(1)} custom-call(f32[1,64,64]{2,1,0:T(8,128)S(1)} %fusion.27), custom_call_target="InvertDiagBlocksLowerTriangular" | custom-call | tf_op jit(solution)/shard_map/triangular_solve/custom-call.2 | solution.py:21
  46.6 2.5 copy.36
  50.3 114.1 %all-gather.2.cloned.1.call-done = bf16[8192,448]{1,0:T(8,128)(2,1)} async-done(((bf16[64,448]{1,0:T(8,128)(2,1)}), bf16[8192,448]{1,0:T(8,128)(2,1)}) %all-gather.2.cloned.1.call-update) | async-done | bytes 7340048 | tf_op jit(solution)/shard_map/all_gather | solution.py:64
  164.4 3.8 %convert_add_fusion = f32[8192,64]{1,0:T(8,128)S(1)} fusion(bf16[8192,448]{1,0:T(8,128)(2,1)} %all-gather.2.cloned.1.call-done), kind=kLoop, calls=%fused_computation.26 | loop fusion | flops 2621440 | bytes 5242880 | tf_op jit(solution)/shard_map/add | solution.py:76
  170.2 7.1 %fusion.44 = f32[64,64]{1,0:T(8,128)S(1)} fusion(f32[8192,64]{1,0:T(8,128)S(1)} %convert_add_fusion), kind=kOutput, calls=%fused_computation.88 | convolution fusion | flops 402653184 | bytes 2113536 | tf_op jit(solution)/shard_map/dot_general | solution.py:16
  177.4 5.8 %cholesky.74 = f32[64,64]{1,0:T(8,128)S(1)} custom-call(f32[64,64]{1,0:T(8,128)S(1)} %fusion.36), custom_call_target="Cholesky" | custom-call | tf_op jit(solution)/shard_map/jit(cholesky)/cholesky | solution.py:34
  184.6 4.9 %custom-call.10 = f32[1,64,64]{1,2,0:T(8,128)S(1)} custom-call(f32[1,64,64]{2,1,0:T(8,128)S(1)} %fusion.24), custom_call_target="InvertDiagBlocksLowerTriangular" | custom-call | tf_op jit(solution)/shard_map/triangular_solve/custom-call.0 | solution.py:33
  190.2 5.8 %cholesky.85 = f32[64,64]{1,0:T(8,128)S(1)} custom-call(f32[64,64]{1,0:T(8,128)S(1)} %fusion.34), custom_call_target="Cholesky" | custom-call | tf_op jit(solution)/shard_map/jit(cholesky)/cholesky | solution.py:38
  197.4 4.9 %custom-call.11 = f32[1,64,64]{1,2,0:T(8,128)S(1)} custom-call(f32[1,64,64]{2,1,0:T(8,128)S(1)} %fusion.25), custom_call_target="InvertDiagBlocksLowerTriangular" | custom-call | tf_op jit(solution)/shard_map/triangular_solve/custom-call.0 | solution.py:37
  202.8 8.5 %fusion.43 = (bf16[8192,64]{0,1:T(8,128)(2,1)S(1)}, f32[8192,64]{0,1:T(8,128)}) fusion(f32[8192,64]{1,0:T(8,128)} %copy-done.1, f32[64,64]{1,0:T(8,128)S(1)} %fusion.47), kind=kOutput, calls=%fused_computation.87 | convolution fusion | flops 403177472 | bytes 5259264 | tf_op jit(solution)/shard_map/dot_general | solution.py:16
  212.4 2.1 slice-done
  215.3 5.6 %fusion.9 = f32[512,320]{0,1:T(8,128)S(1)} fusion(bf16[128,8192]{1,0:T(8,128)(2,1)} %collective-permute-done.2, bf16[128,8192]{1,0:T(8,128)(2,1)} %collective-permute-done.1, bf16[128,8192]{1,0:T(8,128)(2,1)} %collective-permute-done, bf16[128,8192]{1,0:T(8,128)(2,1)S(1)} %bitcast.117, bf16[8192,64]{1,0:T(8,128)(2,1)S(1)} %copy.37, ...), kind=kOutput, calls=%fused_computation.15 | convolution fusion | flops 2728394752 | bytes 14286848 | tf_op jit(solution)/shard_map/dot_general | solution.py:85
  222.8 25.5 %while.23 = (s32[]{:T(128)}, f32[2,2]{1,0:T(2,128)S(1)}, bf16[2,8,512,128]{2,3,1,0:T(8,128)(2,1)}, bf16[2,2,512,128]{3,2,1,0:T(8,128)(2,1)S(1)}, s32[512]{0:T(51...) while((s32[]{:T(128)}, f32[2,2]{1,0:T(2,128)S(1)}, ...), condition=%wide.region_9.13_spmd.clone, body=%wide.region_2.12_spmd.clone.sunk | while | flops 138674192 | bytes 10115450 | solution.py:117
  225.1 10.4 %while.24 = (s32[]{:T(128)}, f32[8,2]{1,0:T(8,128)S(1)}, pred[512,512]{0,1:T(8,128)(4,1)S(1)}, bf16[8,512,128]{2,1,0:T(8,128)(2,1)S(1)}, bf16[2,512,128]{2,1,0:T(8,128)(2,1)S(1)}, /*index=5*/s32[]{:T(128)}, s32[]{:T(128)}) while((s32[]{:T(128)}, f32[8,2]{1,0:T(8,128)S(1)}, pred[512,512]{0,1:T(8,128)(4,1)S(1)}, ...), condition=%wide.region_7.10_spmd, body=%wide.region_3.0_spmd.sunk | while | flops 138412032 | bytes 5132397 | solution.py:114
  237.8 10.4 %while.24 = (s32[]{:T(128)}, f32[8,2]{1,0:T(8,128)S(1)}, pred[512,512]{0,1:T(8,128)(4,1)S(1)}, bf16[8,512,128]{2,1,0:T(8,128)(2,1)S(1)}, bf16[2,512,128]{2,1,0:T(8,128)(2,1)S(1)}, /*index=5*/s32[]{:T(128)}, s32[]{:T(128)}) while((s32[]{:T(128)}, f32[8,2]{1,0:T(8,128)S(1)}, pred[512,512]{0,1:T(8,128)(4,1)S(1)}, ...), condition=%wide.region_7.10_spmd, body=%wide.region_3.0_spmd.sunk | while | flops 138412032 | bytes 5132397 | solution.py:114
  248.9 9.6 %all-to-all-start = ((f32[128,1,2]{2,1,0:T(1,128)}), f32[128,1,2]{2,1,0:T(1,128)S(1)}, u32[]{:S(2)}, u32[]{:S(2)}) async-start(f32[128,1,2]{2,1,0:T(1,128)} %broadcast_in_dim.47), calls=%async_computation | async-start | bytes 131072 | tf_op jit(solution)/shard_map/all_to_all | solution.py:54
  260.5 12.9 %all-to-all-done = f32[128,1,2]{2,1,0:T(1,128)S(1)} async-done(((f32[128,1,2]{2,1,0:T(1,128)}), f32[128,1,2]{2,1,0:T(1,128)S(1)}, u32[]{:S(2)}, u32[]{:S(2)}) %all-to-all-start) | async-done | bytes 1056 | tf_op jit(solution)/shard_map/all_to_all | solution.py:54
  273.6 7.9 %all_to_all.12 = f32[4,1,2]{2,1,0:T(1,128)S(1)} all-to-all(f32[4,1,2]{2,1,0:T(1,128)S(1)} %broadcast_in_dim.48), channel_id=1, replica_groups=mesh['fsdp'=128,'seq'=4] {'seq'}, dimensions={0} | all-to-all | bytes 64 | tf_op jit(solution)/shard_map/all_to_all | solution.py:54
  (140 shorter events, 45.5 us)
Async XLA Ops:
  7.2 13.9 %copy-start = (f32[1024,64]{0,1:T(8,128)S(1)}, f32[1024,64]{0,1:T(8,128)}, u32[]{:S(2)}) copy-start(f32[1024,64]{0,1:T(8,128)} %param.18) | copy-start | bytes 786436
  7.2 39.4 %copy-start.2 = (bf16[1,512,2048]{2,1,0:T(8,128)(2,1)S(1)}, bf16[1,512,2048]{2,1,0:T(8,128)(2,1)}, u32[]{:S(2)}) copy-start(bf16[1,512,2048]{2,1,0:T(8,128)(2,1)} %param.15) | copy-start | bytes 6291460
  7.2 157.3 %all-gather.2.cloned.1.call-start = ((), (), s32[]{:S(2)}) async-start(), calls=%async_computation.2 | async-start | bytes 8454144 | tf_op jit(solution)/shard_map/all_gather | solution.py:64
  9.7 202.8 %collective-permute-start = (bf16[128,8192]{1,0:T(8,128)(2,1)}, bf16[128,8192]{1,0:T(8,128)(2,1)}, u32[]{:S(2)}, u32[]{:S(2)}) collective-permute-start(bf16[128,8192]{1,0:T(8,128)(2,1)} %bitcast.114), channel_id=1, source_target_pairs={{0,1},{1,2},{2,3},{3,0},{4,5},{5,6},{6,7},{7,4},{8,9},{9,10},{10,1... | collective-permute-start | bytes 6291464 | tf_op jit(solution)/shard_map/ppermute | solution.py:70
  13.6 198.8 %collective-permute-start.1 = (bf16[128,8192]{1,0:T(8,128)(2,1)}, bf16[128,8192]{1,0:T(8,128)(2,1)}, u32[]{:S(2)}, u32[]{:S(2)}) collective-permute-start(bf16[128,8192]{1,0:T(8,128)(2,1)} %bitcast.115), channel_id=1, source_target_pairs={{0,2},{1,3},{2,0},{3,1},{4,6},{5,7},{6,4},{7,5},{8,10},{9,11},{10,... | collective-permute-start | bytes 6291464 | tf_op jit(solution)/shard_map/ppermute | solution.py:70
  18.0 194.5 %collective-permute-start.2 = (bf16[128,8192]{1,0:T(8,128)(2,1)}, bf16[128,8192]{1,0:T(8,128)(2,1)}, u32[]{:S(2)}, u32[]{:S(2)}) collective-permute-start(bf16[128,8192]{1,0:T(8,128)(2,1)} %bitcast.116), channel_id=1, source_target_pairs={{0,3},{1,0},{2,1},{3,2},{4,7},{5,4},{6,5},{7,6},{8,11},{9,8},{10,9... | collective-permute-start | bytes 6291464 | tf_op jit(solution)/shard_map/ppermute | solution.py:70
  168.2 2.0 copy-start.1
  212.4 2.2 slice-start
  212.4 2.9 copy-start.4
  222.7 35.8 %copy-start.3 = (f32[1024,64]{0,1:T(8,128)S(1)}, f32[1024,64]{0,1:T(8,128)}, u32[]{:S(2)}) copy-start(f32[1024,64]{0,1:T(8,128)} %convolution_bitcast_fusion) | copy-start | bytes 786436
  248.9 24.5 %all-to-all-start = ((f32[128,1,2]{2,1,0:T(1,128)}), f32[128,1,2]{2,1,0:T(1,128)S(1)}, u32[]{:S(2)}, u32[]{:S(2)}) async-start(f32[128,1,2]{2,1,0:T(1,128)} %broadcast_in_dim.47), calls=%async_computation | async-start | bytes 131072 | tf_op jit(solution)/shard_map/all_to_all | solution.py:54
Sparse Core Ops, SparseCore 0:
  11.1 153.2 all-gather.1
where the time goes:
time: 289 us
  waiting for transfers between devices  127 us (44%)
  other arithmetic  67 us (23%)
  matrix products  36.8 us (13%)
  starting transfers between devices  21 us (7%)
  local copies, waits for them, and re-layouts  14.4 us (5%)
  between operations  14.4 us (5%)
  blocking collectives  7.89 us (3%)
    all_gather x1, waiting for transfers between devices, local(): whole = lax.all_gather(packed, 'fsdp', axis=0, tiled=True)  114 us
    dot_general x9, matrix products, highest(): jnp.dot(left, right, precision=lax.Precision.HIGHEST, preferred_element_t...  20.4 us
    another operation x6, other arithmetic, solve_rows(): lower = jnp.linalg.cholesky(gram)  13 us
    all_to_all x1, waiting for transfers between devices, total_over(): return jnp.sum(lax.all_to_all(spread, axis, 0, 0, tiled=True), axis=0)  12.9 us
    ppermute x3, starting transfers between devices, local(): lax.ppermute(x_local, 'seq', [(i, (i + shift) % n_seq) for i in range(n_s...  11.4 us
    another operation x4, other arithmetic, solve_rows(): lax.linalg.triangular_solve(lower, rows, left_side=False, lower=True, tra...  11.1 us
    all_to_all x1, starting transfers between devices, total_over(): return jnp.sum(lax.all_to_all(spread, axis, 0, 0, tiled=True), axis=0)  9.62 us
    reduce_sum x16, other arithmetic, one_query_head(): jnp.sum(jnp.where(causal[None], jnp.exp(scores - top[..., None]), 0.0), a...  9.15 us
  transfers between devices with their start and end apart: 5, of which 2 were waited for; matrix products, arithmetic and copies ran while one was open for 27% of the time, Pallas kernels for 0%

commit v1 on v0

--- a/solution.py
+++ b/solution.py
@@ -61,7 +61,12 @@
     slice_width = key_weight.shape[1]
     rows = u_factor.shape[0]
     packed = jnp.concatenate([key_weight] + split3(u_factor), axis=1)
-    whole = lax.all_gather(packed, "fsdp", axis=0, tiled=True)
+    whole = jnp.concatenate(
+        jax.lax.all_to_all(
+            jnp.stack([packed for _ in range(jax.lax.axis_size("fsdp"))], axis=0), "fsdp", 0, 0
+        ),
+        axis=0,
+    )
     x_local = tokens[0]
     chunk = x_local.shape[0]
     chunks = [x_local]

time: 289 us -> 515 us (1.78)
  waiting for transfers between devices: 127 us -> 337 us
  starting transfers between devices: 21 us -> 43.9 us
  between operations: 14.4 us -> 0.99 us
  local copies, waits for them, and re-layouts: 14.4 us -> 20.2 us
    all_to_all x0 -> x1, waiting for transfers between devices: none -> 324 us  [local(): jax.lax.all_to_all(jnp.stack([packed for _ in range(jax.lax.axis_size('fs...]
    all_gather x1 -> x0, waiting for transfers between devices: 114 us -> none  [local(): whole = lax.all_gather(packed, 'fsdp', axis=0, tiled=True)]
    all_to_all x0 -> x1, starting transfers between devices: none -> 21 us  [local(): jax.lax.all_to_all(jnp.stack([packed for _ in range(jax.lax.axis_size('fs...]
  transfers between devices with their start and end apart: 5 -> 5, of which waited for: 2 -> 2; matrix products, arithmetic and copies ran while one was open for 27% -> 16% of each run, Pallas kernels for 0% -> 0%
where the time goes in v1:
time: 515 us; the launch traced here: 514 us
  waiting for transfers between devices  337 us (65%)
  other arithmetic  66.2 us (13%)
  starting transfers between devices  43.9 us (9%)
  matrix products  37.5 us (7%)
  local copies, waits for them, and re-layouts  20.2 us (4%)
  blocking collectives  7.94 us (2%)
    all_to_all x1, waiting for transfers between devices, local(): jax.lax.all_to_all(jnp.stack([packed for _ in range(jax.lax.axis_size('fs...  324 us
    all_to_all x1, starting transfers between devices, local(): jax.lax.all_to_all(jnp.stack([packed for _ in range(jax.lax.axis_size('fs...  21 us
    dot_general x9, matrix products, highest(): jnp.dot(left, right, precision=lax.Precision.HIGHEST, preferred_element_t...  20.3 us
    another operation x6, other arithmetic, solve_rows(): lower = jnp.linalg.cholesky(gram)  13 us
    all_to_all x1, waiting for transfers between devices, total_over(): return jnp.sum(lax.all_to_all(spread, axis, 0, 0, tiled=True), axis=0)  12.9 us
    all_to_all x1, starting transfers between devices, total_over(): return jnp.sum(lax.all_to_all(spread, axis, 0, 0, tiled=True), axis=0)  12.2 us
    another operation x4, other arithmetic, solve_rows(): lax.linalg.triangular_solve(lower, rows, left_side=False, lower=True, tra...  11.1 us
    ppermute x3, starting transfers between devices, local(): lax.ppermute(x_local, 'seq', [(i, (i + shift) % n_seq) for i in range(n_s...  10.7 us
  transfers between devices with their start and end apart: 5, of which 2 were waited for; matrix products, arithmetic and copies ran while one was open for 16% of the time, Pallas kernels for 0%

profile of v1, /device:TPU:1, one launch (start us, length us, event | category | flops | bytes accessed | tf_op | source)
XLA Modules:
  0.0 514.2 jit_solution(14461433863919634058)
XLA Ops:
  2.3 4.3 stack.8
  6.6 21.0 %all-to-all-start = ((bf16[128,64,448]{2,1,0:T(8,128)(2,1)}), bf16[128,64,448]{2,1,0:T(8,128)(2,1)}, u32[]{:S(2)}, u32[]{:S(2)}) async-start(bf16[128,64,448]{2,1,0:T(8,128)(2,1)} %stack.8), calls=%async_computation | async-start | bytes 16777216 | tf_op jit(solution)/shard_map/all_to_all | solution.py:65
  27.6 3.3 collective-permute-start
  30.9 4.4 collective-permute-start.1
  38.8 5.8 %cholesky.96 = f32[64,64]{1,0:T(8,128)S(1)} custom-call(f32[64,64]{1,0:T(8,128)S(1)} %fusion.32), custom_call_target="Cholesky" | custom-call | tf_op jit(solution)/shard_map/jit(cholesky)/cholesky | solution.py:20
  46.0 4.9 custom-call.12
  51.8 5.8 %cholesky.107 = f32[64,64]{1,0:T(8,128)S(1)} custom-call(f32[64,64]{1,0:T(8,128)S(1)} %fusion.30), custom_call_target="Cholesky" | custom-call | tf_op jit(solution)/shard_map/jit(cholesky)/cholesky | solution.py:20
  58.9 4.9 custom-call.13
  67.6 324.2 %all-to-all-done = bf16[128,64,448]{2,1,0:T(8,128)(2,1)} async-done(((bf16[128,64,448]{2,1,0:T(8,128)(2,1)}), bf16[128,64,448]{2,1,0:T(8,128)(2,1)}, u32[]{:S(2)}, u32[]{:S(2)}) %all-to-all-start) | async-done | bytes 7340064 | tf_op jit(solution)/shard_map/all_to_all | solution.py:65
  391.8 3.8 convert_add_fusion
  397.5 7.1 %fusion.44 = f32[64,64]{1,0:T(8,128)S(1)} fusion(f32[8192,64]{1,0:T(8,128)S(1)} %convert_add_fusion), kind=kOutput, calls=%fused_computation.88 | convolution fusion | flops 402653184 | bytes 2113536 | tf_op jit(solution)/shard_map/dot_general | solution.py:16
  404.7 5.8 %cholesky.74 = f32[64,64]{1,0:T(8,128)S(1)} custom-call(f32[64,64]{1,0:T(8,128)S(1)} %fusion.36), custom_call_target="Cholesky" | custom-call | tf_op jit(solution)/shard_map/jit(cholesky)/cholesky | solution.py:34
  411.9 4.9 custom-call.10
  417.1 4.4 slice.35
  421.9 5.8 %cholesky.85 = f32[64,64]{1,0:T(8,128)S(1)} custom-call(f32[64,64]{1,0:T(8,128)S(1)} %fusion.34), custom_call_target="Cholesky" | custom-call | tf_op jit(solution)/shard_map/jit(cholesky)/cholesky | solution.py:38
  429.1 4.9 custom-call.11
  434.7 8.3 %fusion.43 = (bf16[8192,64]{0,1:T(8,128)(2,1)S(1)}, f32[8192,64]{0,1:T(8,128)}) fusion(f32[8192,64]{1,0:T(8,128)} %copy-done.1, f32[64,64]{1,0:T(8,128)S(1)} %fusion.47), kind=kOutput, calls=%fused_computation.87 | convolution fusion | flops 403177472 | bytes 5259264 | tf_op jit(solution)/shard_map/dot_general | solution.py:16
  444.1 6.3 %fusion.9 = f32[512,320]{0,1:T(8,128)S(1)} fusion(bf16[128,8192]{1,0:T(8,128)(2,1)} %collective-permute-done.2, bf16[128,8192]{1,0:T(8,128)(2,1)} %collective-permute-done.1, bf16[128,8192]{1,0:T(8,128)(2,1)} %collective-permute-done, bf16[128,8192]{1,0:T(8,128)(2,1)} %bitcast.118, bf16[8192,64]{1,0:T(8,128)(2,1)S(1)} %copy.61, bf16[8192,256]{1,0:T(8,128)(2,1)} %slice.35), kind=kOutput, calls=%fused_computation.15 | convolution fusion | flops 2728394752 | bytes 14286848 | tf_op jit(solution)/shard_map/dot_general | solution.py:90
  452.4 25.5 %while.23 = (s32[]{:T(128)}, f32[2,2]{1,0:T(2,128)S(1)}, bf16[2,8,512,128]{2,3,1,0:T(8,128)(2,1)}, bf16[2,2,512,128]{3,2,1,0:T(8,128)(2,1)S(1)}, s32[512]{0:T(51...) while((s32[]{:T(128)}, f32[2,2]{1,0:T(2,128)S(1)}, ...), condition=%wide.region_9.13_spmd.clone, body=%wide.region_2.12_spmd.clone.sunk | while | flops 138674192 | bytes 10115450 | solution.py:122
  454.7 10.4 %while.24 = (s32[]{:T(128)}, f32[8,2]{1,0:T(8,128)S(1)}, pred[512,512]{0,1:T(8,128)(4,1)S(1)}, bf16[8,512,128]{2,1,0:T(8,128)(2,1)S(1)}, bf16[2,512,128]{2,1,0:T(8,128)(2,1)S(1)}, /*index=5*/s32[]{:T(128)}, s32[]{:T(128)}) while((s32[]{:T(128)}, f32[8,2]{1,0:T(8,128)S(1)}, pred[512,512]{0,1:T(8,128)(4,1)S(1)}, ...), condition=%wide.region_7.10_spmd, body=%wide.region_3.0_spmd.sunk | while | flops 138412032 | bytes 5132397 | solution.py:119
  467.4 10.4 %while.24 = (s32[]{:T(128)}, f32[8,2]{1,0:T(8,128)S(1)}, pred[512,512]{0,1:T(8,128)(4,1)S(1)}, bf16[8,512,128]{2,1,0:T(8,128)(2,1)S(1)}, bf16[2,512,128]{2,1,0:T(8,128)(2,1)S(1)}, /*index=5*/s32[]{:T(128)}, s32[]{:T(128)}) while((s32[]{:T(128)}, f32[8,2]{1,0:T(8,128)S(1)}, pred[512,512]{0,1:T(8,128)(4,1)S(1)}, ...), condition=%wide.region_7.10_spmd, body=%wide.region_3.0_spmd.sunk | while | flops 138412032 | bytes 5132397 | solution.py:119
  478.5 12.2 %all-to-all-start.1 = ((f32[128,1,2]{2,1,0:T(1,128)}), f32[128,1,2]{2,1,0:T(1,128)S(1)}, u32[]{:S(2)}, u32[]{:S(2)}) async-start(f32[128,1,2]{2,1,0:T(1,128)} %broadcast_in_dim.47), calls=%async_computation.1 | async-start | bytes 131072 | tf_op jit(solution)/shard_map/all_to_all | solution.py:54
  492.7 12.9 %all-to-all-done.1 = f32[128,1,2]{2,1,0:T(1,128)S(1)} async-done(((f32[128,1,2]{2,1,0:T(1,128)}), f32[128,1,2]{2,1,0:T(1,128)S(1)}, u32[]{:S(2)}, u32[]{:S(2)}) %all-to-all-start.1) | async-done | bytes 1056 | tf_op jit(solution)/shard_map/all_to_all | solution.py:54
  505.8 7.9 %all_to_all.17 = f32[4,1,2]{2,1,0:T(1,128)S(1)} all-to-all(f32[4,1,2]{2,1,0:T(1,128)S(1)} %broadcast_in_dim.48), channel_id=1, replica_groups=mesh['fsdp'=128,'seq'=4] {'seq'}, dimensions={0} | all-to-all | bytes 64 | tf_op jit(solution)/shard_map/all_to_all | solution.py:54
  (137 shorter events, 49.8 us)
Async XLA Ops:
  0.6 37.7 %copy-start = (f32[1024,64]{0,1:T(8,128)S(1)}, f32[1024,64]{0,1:T(8,128)}, u32[]{:S(2)}) copy-start(f32[1024,64]{0,1:T(8,128)} %param.18) | copy-start | bytes 786436
  6.6 385.2 %all-to-all-start = ((bf16[128,64,448]{2,1,0:T(8,128)(2,1)}), bf16[128,64,448]{2,1,0:T(8,128)(2,1)}, u32[]{:S(2)}, u32[]{:S(2)}) async-start(bf16[128,64,448]{2,1,0:T(8,128)(2,1)} %stack.8), calls=%async_computation | async-start | bytes 16777216 | tf_op jit(solution)/shard_map/all_to_all | solution.py:65
  27.6 36.3 %copy-start.2 = (bf16[1,512,2048]{2,1,0:T(8,128)(2,1)S(1)}, bf16[1,512,2048]{2,1,0:T(8,128)(2,1)}, u32[]{:S(2)}) copy-start(bf16[1,512,2048]{2,1,0:T(8,128)(2,1)} %param.15) | copy-start | bytes 6291460
  27.6 416.5 %collective-permute-start = (bf16[128,8192]{1,0:T(8,128)(2,1)}, bf16[128,8192]{1,0:T(8,128)(2,1)}, u32[]{:S(2)}, u32[]{:S(2)}) collective-permute-start(bf16[128,8192]{1,0:T(8,128)(2,1)} %bitcast.115), channel_id=1, source_target_pairs={{0,1},{1,2},{2,3},{3,0},{4,5},{5,6},{6,7},{7,4},{8,9},{9,10},{10,1... | collective-permute-start | bytes 6291464 | tf_op jit(solution)/shard_map/ppermute | solution.py:75
  30.9 413.3 %collective-permute-start.1 = (bf16[128,8192]{1,0:T(8,128)(2,1)}, bf16[128,8192]{1,0:T(8,128)(2,1)}, u32[]{:S(2)}, u32[]{:S(2)}) collective-permute-start(bf16[128,8192]{1,0:T(8,128)(2,1)} %bitcast.116), channel_id=1, source_target_pairs={{0,2},{1,3},{2,0},{3,1},{4,6},{5,7},{6,4},{7,5},{8,10},{9,11},{10,... | collective-permute-start | bytes 6291464 | tf_op jit(solution)/shard_map/ppermute | solution.py:75
  35.2 408.9 %collective-permute-start.2 = (bf16[128,8192]{1,0:T(8,128)(2,1)}, bf16[128,8192]{1,0:T(8,128)(2,1)}, u32[]{:S(2)}, u32[]{:S(2)}) collective-permute-start(bf16[128,8192]{1,0:T(8,128)(2,1)} %bitcast.117), channel_id=1, source_target_pairs={{0,3},{1,0},{2,1},{3,2},{4,7},{5,4},{6,5},{7,6},{8,11},{9,8},{10,9... | collective-permute-start | bytes 6291464 | tf_op jit(solution)/shard_map/ppermute | solution.py:75
  395.6 2.0 copy-start.1
  452.4 38.4 %copy-start.3 = (f32[1024,64]{0,1:T(8,128)S(1)}, f32[1024,64]{0,1:T(8,128)}, u32[]{:S(2)}) copy-start(f32[1024,64]{0,1:T(8,128)} %convolution_bitcast_fusion) | copy-start | bytes 786436
  478.5 27.1 %all-to-all-start.1 = ((f32[128,1,2]{2,1,0:T(1,128)}), f32[128,1,2]{2,1,0:T(1,128)S(1)}, u32[]{:S(2)}, u32[]{:S(2)}) async-start(f32[128,1,2]{2,1,0:T(1,128)} %broadcast_in_dim.47), calls=%async_computation.1 | async-start | bytes 131072 | tf_op jit(solution)/shard_map/all_to_all | solution.py:54
